TPU v7x, 512 devices: a whole 4x4x16 slice. The times are simulated.
512 devices in a mesh: tm: 128 (over z, y, core), chan: 4 (over x).
Axes of the slice: x: 4, y: 4, z: 16, core: 2. Of those that a mesh axis runs over, the one named last changes fastest.
Arguments:
- series: bfloat16 [32768, 512], P('tm', 'chan'), may hold values from -6 to 6
- proj_weight: bfloat16 [512, 3, 512], P(None, None, 'chan'), may hold values from -0.25 to 0.25
- proj_bias: float32 [3, 512], P(None, 'chan'), may hold values from -6 to 6
- short_taps: float32 [3, 3, 512], P(None, None, 'chan'), may hold values from -6 to 6
- short_bias: float32 [3, 512], P(None, 'chan'), may hold values from -6 to 6
- spectrum: float32 [2, 128, 2, 256, 512], P(None, 'tm', None, None, 'chan'), may hold values from -6 to 6
- skip_gain: float32 [512], P('chan'), may hold values from -6 to 6
- out_weight: bfloat16 [512, 512], replicated, may hold values from -0.25 to 0.25
- out_bias: float32 [512], P('chan'), may hold values from -6 to 6
Outputs:
- mixed_out: bfloat16 [32768, 512], P('tm', 'chan')
All inputs are finite; a program needn't handle non-finite values.
Results may differ from a plain program's by a relative error of at most 0.009.
Values may be sent and summed in bfloat16 or wider, within the bound.
No kernel may reach another device: no remote copies, remote signals or barrier semaphores. Data moves between devices by JAX's collectives and lax.ppermute only.
A program may use at most 64 MiB of HBM per device.

v0:
```python
import math
import jax
import jax.numpy as jnp
import numpy as np
from jax import lax
from jax.sharding import PartitionSpec as P

HI = lax.Precision.HIGHEST


def from_behind(array, axis, by):
    length = lax.axis_size(axis)
    pairs = [(i, i + by) for i in range(length) if 0 <= i + by < length]
    return lax.ppermute(array, axis, pairs)


def reverse_bits_np(values, digits):
    result = np.zeros_like(values)
    for bit_level in range(digits):
        result = result | (values >> bit_level & 1) << digits - 1 - bit_level
    return result


def dft_tables(tm_count, steps_dev):
    rows = 2 * tm_count
    digits = tm_count.bit_length() - 1
    r = np.arange(rows)
    k1 = 2 * reverse_bits_np(r // 2, digits) + r % 2
    m = np.arange(tm_count)
    t = np.arange(steps_dev)
    b = np.arange(steps_dev)
    period = rows * steps_dev
    ang1 = 2 * np.pi * (k1[:, None] * m[None, :] % rows) / rows
    ang2 = 2 * np.pi * (t[:, None] * b[None, :] % steps_dev) / steps_dev
    angt = 2 * np.pi * (k1[:, None] * t[None, :] % period) / period
    f32 = lambda a: jnp.asarray(a.astype(np.float32))
    return dict(
        c1=f32(np.cos(ang1)),
        s1=f32(np.sin(ang1)),
        c2=f32(np.cos(ang2)),
        s2=f32(np.sin(ang2)),
        ct=f32(np.cos(angt)),
        st=f32(np.sin(angt)),
        period=period,
    )


def mm(a, b):
    return jnp.dot(a, b, precision=HI, preferred_element_type=jnp.float32)


def long_conv(x, h, tab):
    c1, s1, c2, s2, ct, st = (tab[k] for k in ("c1", "s1", "c2", "s2", "ct", "st"))
    ar = mm(c1, x)
    ai = -mm(s1, x)
    tr = ar * ct + ai * st
    ti = ai * ct - ar * st
    zr = mm(tr, c2) + mm(ti, s2)
    zi = mm(ti, c2) - mm(tr, s2)
    yr = h[0] * zr - h[1] * zi
    yi = h[0] * zi + h[1] * zr
    br = mm(yr, c2) - mm(yi, s2)
    bi = mm(yi, c2) + mm(yr, s2)
    ur = br * ct - bi * st
    ui = bi * ct + br * st
    y = lax.dot_general(
        c1, ur, (((0,), (0,)), ((), ())), precision=HI, preferred_element_type=jnp.float32
    )
    y = y - lax.dot_general(
        s1, ui, (((0,), (0,)), ((), ())), precision=HI, preferred_element_type=jnp.float32
    )
    return y * (1.0 / tab["period"])


def shards(
    series,
    proj_weight,
    proj_bias,
    short_taps,
    short_bias,
    spectrum,
    skip_gain,
    out_weight,
    out_bias,
):
    steps_dev = series.shape[0]
    model_width = proj_weight.shape[0]
    channels = proj_weight.shape[2]
    tm_count = lax.axis_size("tm")
    tab = dft_tables(tm_count, steps_dev)
    flat_weight = proj_weight.reshape(model_width, 3 * channels)
    projected = jnp.dot(
        lax.all_gather(series, "chan", axis=1, tiled=True),
        flat_weight,
        preferred_element_type=jnp.float32,
    )
    projected = (projected.reshape(steps_dev, 3, channels) + proj_bias).astype(jnp.bfloat16)
    taps_count = short_taps.shape[0]
    earlier = from_behind(projected[steps_dev - taps_count + 1 :], "tm", 1)
    extended = jnp.concatenate([earlier, projected], 0).astype(jnp.float32)
    streams = short_bias + short_taps[0] * extended[taps_count - 1 :]
    for offset in range(1, taps_count):
        streams = (
            streams
            + short_taps[offset]
            * extended[taps_count - 1 - offset : taps_count - 1 - offset + steps_dev]
        )
    streams = streams.astype(jnp.bfloat16)
    gate_out = streams[:, 0]
    mixed_in = (streams[:, 1].astype(jnp.float32) * streams[:, 2].astype(jnp.float32)).astype(
        jnp.bfloat16
    )
    pair = jnp.stack([mixed_in, gate_out])[:, None]
    pair = lax.all_to_all(pair, "tm", 3, 1, tiled=True)
    signal_bf = pair[0, :, :, 0]
    gate_own = pair[1, :, :, 0].astype(jnp.float32)
    h = lax.all_to_all(spectrum, "tm", 4, 1, tiled=True)
    h = h.reshape(2, 2 * tm_count, steps_dev)
    signal = signal_bf.astype(jnp.float32)
    convolved = long_conv(signal, h, tab)
    skip = lax.dynamic_index_in_dim(skip_gain, lax.axis_index("tm"), 0, keepdims=False)
    gated = ((convolved + skip * signal) * gate_own).astype(jnp.bfloat16)
    gated = lax.all_to_all(gated[:, :, None], "tm", 0, 2, tiled=True)
    gated = lax.all_gather(gated[0], "chan", axis=1, tiled=True)
    column_start = lax.axis_index("chan") * channels
    weight_cols = lax.dynamic_slice_in_dim(out_weight, column_start, channels, 1)
    mixed_out = jnp.dot(gated, weight_cols, preferred_element_type=jnp.float32) + out_bias
    return mixed_out.astype(jnp.bfloat16)


def solution(mesh):
    return jax.shard_map(
        shards,
        mesh=mesh,
        in_specs=(
            P("tm", "chan"),
            P(None, None, "chan"),
            P(None, "chan"),
            P(None, None, "chan"),
            P(None, "chan"),
            P(None, "tm", None, None, "chan"),
            P("chan"),
            P(),
            P("chan"),
        ),
        out_specs=P("tm", "chan"),
        check_vma=False,
    )
```

profile of v0, /device:TPU:2, one launch (start us, length us, event | category | flops | bytes accessed | tf_op | source)
XLA Modules:
  0.0 140.7 jit_solution(8496077110473266639)
XLA Ops:
  0.0 1.2 copy.32
  1.3 15.2 %all_gather.6 = bf16[256,512]{1,0:T(8,128)(2,1)S(1)} all-gather(bf16[256,128]{1,0:T(8,128)(2,1)S(1)} %copy-done.13), channel_id=1, replica_groups=mesh['tm'=128,'chan'=4] {'chan'}, dimensions={1}, use_global_device_ids=true | all-gather | bytes 327680 | tf_op jit(solution)/shard_map/all_gather | solution.py:93
  16.4 0.3 fusion
  16.8 1.3 collective-permute-start
  18.1 0.8 collective-permute-done
  18.9 0.7 copy-done.16
  19.6 0.1 fusion.9
  19.8 0.8 copy.33
  20.6 20.5 %all-to-all-start.1 = ((bf16[2,1,256,128]{2,0,1,3:T(2,128)(2,1)}), bf16[2,1,256,128]{2,0,1,3:T(2,128)(2,1)S(1)}, u32[]{:S(2)}, u32[]{:S(2)}) async-start(bf16[2,1,256,128]{2,0,1,3:T(2,128)(2,1)} %copy.33), calls=%async_computation.1 | async-start | bytes 262144 | tf_op jit(solution)/shard_map/all_to_all | solution.py:114
  41.1 1.0 copy.31
  42.1 14.4 %all-to-all-done.1 = bf16[2,1,256,128]{2,0,1,3:T(2,128)(2,1)S(1)} async-done(((bf16[2,1,256,128]{2,0,1,3:T(2,128)(2,1)}), bf16[2,1,256,128]{2,0,1,3:T(2,128)(2,1)S(1)}, u32[]{:S(2)}, u32[]{:S(2)}) %all-to-all-start.1) | async-done | bytes 131104 | tf_op jit(solution)/shard_map/all_to_all | solution.py:114
  56.5 7.8 %all-to-all-start = ((f32[2,1,2,256,128]{3,2,1,0,4:T(2,128)}), f32[2,1,2,256,128]{3,2,1,0,4:T(2,128)S(1)}, u32[]{:S(2)}, u32[]{:S(2)}) async-start(f32[2,1,2,256,128]{3,2,1,0,4:T(2,128)} %copy.31), calls=%async_computation | async-start | bytes 1048576 | tf_op jit(solution)/shard_map/all_to_all | solution.py:117
  64.4 0.6 copy-done.18
  65.0 0.6 dynamic_slice.7
  65.6 0.1 copy.34
  65.7 0.8 copy-done.11
  66.5 0.3 convolution_negate_fusion
  66.8 0.3 fusion.26
  67.1 0.4 copy-done.3
  67.5 0.1 copy-done.6
  67.5 0.2 copy-done.2
  67.8 0.4 fusion.23
  68.2 0.6 copy-done.1
  68.7 0.1 copy-done.5
  68.8 1.1 fusion.24
  69.9 0.4 convolution_add_fusion.2
  70.3 24.9 %all-to-all-done = f32[2,1,2,256,128]{3,2,1,0,4:T(2,128)S(1)} async-done(((f32[2,1,2,256,128]{3,2,1,0,4:T(2,128)}), f32[2,1,2,256,128]{3,2,1,0,4:T(2,128)S(1)}, u32[]{:S(2)}, u32[]{:S(2)}) %all-to-all-start) | async-done | bytes 524320 | tf_op jit(solution)/shard_map/all_to_all | solution.py:117
  95.2 0.2 fusion.28
  95.4 0.2 squeeze.23
  95.6 0.2 squeeze.21
  95.8 0.8 copy-done.7
  96.6 1.4 multiply_subtract_fusion
  97.9 0.4 fusion.30
  98.3 0.4 fusion.29
  98.7 0.4 convolution_add_fusion.1
  99.1 0.4 convolution_subtract_fusion
  99.5 0.5 copy-done.9
  100.0 0.6 fusion.18
  100.6 0.3 copy-done.12
  100.9 1.2 fusion.7
  102.1 0.1 copy.36
  102.3 0.5 broadcast.5
  102.8 1.0 reduce
  103.8 0.7 reshape.55
  104.5 9.0 %all-to-all-start.2 = ((bf16[128,2,128]{2,1,0:T(2,128)(2,1)}), bf16[128,2,128]{2,1,0:T(2,128)(2,1)S(1)}, u32[]{:S(2)}, u32[]{:S(2)}) async-start(bf16[128,2,128]{2,1,0:T(2,128)(2,1)} %reshape.55), calls=%async_computation.2 | async-start | bytes 131072 | tf_op jit(solution)/shard_map/all_to_all | solution.py:123
  113.5 14.5 %all-to-all-done.2 = bf16[128,2,128]{2,1,0:T(2,128)(2,1)S(1)} async-done(((bf16[128,2,128]{2,1,0:T(2,128)(2,1)}), bf16[128,2,128]{2,1,0:T(2,128)(2,1)S(1)}, u32[]{:S(2)}, u32[]{:S(2)}) %all-to-all-start.2) | async-done | bytes 65568 | tf_op jit(solution)/shard_map/all_to_all | solution.py:123
  128.0 11.8 %all-gather = bf16[1,256,512,1]{1,2,3,0:T(8,128)(2,1)S(1)} all-gather(bf16[1,256,128,1]{1,2,3,0:T(8,128)(2,1)S(1)} %bitcast.98), channel_id=2, replica_groups=mesh['tm'=128,'chan'=4] {'chan'}, dimensions={2}, use_global_device_ids=true | all-gather | bytes 327680 | tf_op jit(solution)/shard_map/all_gather | solution.py:124
  139.8 0.9 fusion.6
  (35 shorter events, 0.2 us)
Async XLA Ops:
  0.0 139.8 %copy-start = (bf16[512,512]{1,0:T(8,128)(2,1)S(1)}, bf16[512,512]{1,0:T(8,128)(2,1)}, u32[]{:S(2)}) copy-start(bf16[512,512]{1,0:T(8,128)(2,1)} %param.22) | copy-start | bytes 1572868
  0.0 1.2 copy-start.13
  1.2 15.2 %copy-start.15 = (f32[3,128]{1,0:T(4,128)S(1)}, f32[3,128]{1,0:T(4,128)}, u32[]{:S(2)}) copy-start(f32[3,128]{1,0:T(4,128)} %param.17) | copy-start | bytes 4612
  16.4 1.6 %copy-start.14 = (f32[3,3,128]{2,1,0:T(4,128)S(1)}, f32[3,3,128]{2,1,0:T(4,128)}, u32[]{:S(2)}) copy-start(f32[3,3,128]{2,1,0:T(4,128)} %param.18) | copy-start | bytes 13828
  16.8 2.1 %collective-permute-start = (bf16[2,3,128]{2,0,1:T(2,128)(2,1)S(1)}, bf16[2,3,128]{2,0,1:T(2,128)(2,1)S(1)}, u32[]{:S(2)}, u32[]{:S(2)}) collective-permute-start(bf16[2,3,128]{2,0,1:T(2,128)(2,1)S(1)} %slice.63), channel_id=1, source_target_pairs={{0,4},{4,8},{8,12},{12,16},{16,20},{20,24},{24,28},{28,32},{32,36}... | collective-permute-start | bytes 4616 | tf_op jit(solution)/shard_map/ppermute | solution.py:14
  18.9 0.7 copy-start.16
  19.8 21.4 %copy-start.10 = (f32[2,1,2,256,128]{4,3,2,1,0:T(8,128)S(1)}, f32[2,1,2,256,128]{4,3,2,1,0:T(8,128)}, u32[]{:S(2)}) copy-start(f32[2,1,2,256,128]{4,3,2,1,0:T(8,128)} %param.20) | copy-start | bytes 1572868
  20.6 35.9 %all-to-all-start.1 = ((bf16[2,1,256,128]{2,0,1,3:T(2,128)(2,1)}), bf16[2,1,256,128]{2,0,1,3:T(2,128)(2,1)S(1)}, u32[]{:S(2)}, u32[]{:S(2)}) async-start(bf16[2,1,256,128]{2,0,1,3:T(2,128)(2,1)} %copy.33), calls=%async_computation.1 | async-start | bytes 262144 | tf_op jit(solution)/shard_map/all_to_all | solution.py:114
  56.5 38.7 %all-to-all-start = ((f32[2,1,2,256,128]{3,2,1,0,4:T(2,128)}), f32[2,1,2,256,128]{3,2,1,0,4:T(2,128)S(1)}, u32[]{:S(2)}, u32[]{:S(2)}) async-start(f32[2,1,2,256,128]{3,2,1,0,4:T(2,128)} %copy.31), calls=%async_computation | async-start | bytes 1048576 | tf_op jit(solution)/shard_map/all_to_all | solution.py:117
  64.3 0.7 copy-start.18
  65.6 0.9 copy-start.11
  65.6 1.2 copy-start.8
  66.5 1.0 copy-start.3
  66.5 1.0 copy-start.6
  66.8 1.0 copy-start.2
  67.8 0.9 copy-start.1
  67.8 1.0 copy-start.5
  68.8 1.1 copy-start.4
  95.6 1.0 copy-start.7
  99.1 0.9 copy-start.9
  100.0 0.9 copy-start.12
  104.5 23.5 %all-to-all-start.2 = ((bf16[128,2,128]{2,1,0:T(2,128)(2,1)}), bf16[128,2,128]{2,1,0:T(2,128)(2,1)S(1)}, u32[]{:S(2)}, u32[]{:S(2)}) async-start(bf16[128,2,128]{2,1,0:T(2,128)(2,1)} %reshape.55), calls=%async_computation.2 | async-start | bytes 131072 | tf_op jit(solution)/shard_map/all_to_all | solution.py:123
  128.0 11.8 %copy-start.17 = (f32[128]{0:T(128)S(1)}, f32[128]{0:T(128)}, u32[]{:S(2)}) copy-start(f32[128]{0:T(128)} %param.23) | copy-start | bytes 1540
where the time goes:
time: 141 us
  waiting for transfers between devices  54.5 us (39%)
  starting transfers between devices  38.6 us (27%)
  blocking collectives  26.9 us (19%)
  local copies, waits for them, and re-layouts  10.7 us (8%)
  matrix products  8.38 us (6%)
    all_to_all x1, waiting for transfers between devices, shards(): h = lax.all_to_all(spectrum, 'tm', 4, 1, tiled=True)  24.9 us
    all_to_all x1, starting transfers between devices, shards(): pair = lax.all_to_all(pair, 'tm', 3, 1, tiled=True)  20.5 us
    all_gather x1, blocking collectives, shards(): lax.all_gather(series, 'chan', axis=1, tiled=True)  15.2 us
    all_to_all x1, waiting for transfers between devices, shards(): gated = lax.all_to_all(gated[:, :, None], 'tm', 0, 2, tiled=True)  14.5 us
    all_to_all x1, waiting for transfers between devices, shards(): pair = lax.all_to_all(pair, 'tm', 3, 1, tiled=True)  14.4 us
    all_gather x1, blocking collectives, shards(): gated = lax.all_gather(gated[0], 'chan', axis=1, tiled=True)  11.8 us
    all_to_all x1, starting transfers between devices, shards(): gated = lax.all_to_all(gated[:, :, None], 'tm', 0, 2, tiled=True)  9.02 us
    unnamed x44, local copies, waits for them, and re-layouts  8.47 us
  transfers between devices with their start and end apart: 4, of which 4 were waited for; matrix products, arithmetic and copies ran while one was open for 3% of the time, Pallas kernels for 0%

commit v1 on v0

--- a/solution.py
+++ b/solution.py
@@ -1,3 +1,4 @@
+import functools
 import math
 import jax
 import jax.numpy as jnp
@@ -6,6 +7,35 @@
 from jax.sharding import PartitionSpec as P
 
 HI = lax.Precision.HIGHEST
+
+
+def arrays_produce(slab_in, axis_no):
+    w1 = lax.axis_size("chan")
+    prior = lax.axis_index("chan")
+    z_new, m_next, current_arr = (w1, prior, slab_in.shape[axis_no])
+    stack_in = [(no, (no + 1) % z_new) for no in range(z_new)]
+    windows = [(no, (no - 1) % z_new) for no in range(z_new)]
+    h_now = jnp.zeros(
+        (*slab_in.shape[:axis_no], z_new * current_arr, *slab_in.shape[axis_no + 1 :]),
+        slab_in.dtype,
+    )
+    h_now = lax.dynamic_update_slice_in_dim(h_now, slab_in, m_next * current_arr, axis=axis_no)
+    field_out = mat_out = slab_in
+    r_now = z_new // 2
+    for pp in range(1, r_now + 1):
+        field_out = lax.ppermute(field_out, axis_name="chan", perm=stack_in)
+        h_now = lax.dynamic_update_slice_in_dim(
+            h_now, field_out, (m_next - pp) % z_new * current_arr, axis=axis_no
+        )
+        if pp < z_new - r_now:
+            mat_out = lax.ppermute(mat_out, axis_name="chan", perm=windows)
+            h_now = lax.dynamic_update_slice_in_dim(
+                h_now, mat_out, (m_next + pp) % z_new * current_arr, axis=axis_no
+            )
+    return h_now
+
+
+_map_state = functools.partial(arrays_produce, axis_no=1)
 
 
 def from_behind(array, axis, by):
@@ -121,7 +151,7 @@
     skip = lax.dynamic_index_in_dim(skip_gain, lax.axis_index("tm"), 0, keepdims=False)
     gated = ((convolved + skip * signal) * gate_own).astype(jnp.bfloat16)
     gated = lax.all_to_all(gated[:, :, None], "tm", 0, 2, tiled=True)
-    gated = lax.all_gather(gated[0], "chan", axis=1, tiled=True)
+    gated = _map_state(gated[0])
     column_start = lax.axis_index("chan") * channels
     weight_cols = lax.dynamic_slice_in_dim(out_weight, column_start, channels, 1)
     mixed_out = jnp.dot(gated, weight_cols, preferred_element_type=jnp.float32) + out_bias

time: 141 us -> 143 us (1.014)
  the two profiles are of different devices: /device:TPU:2 before, /device:TPU:32 now
where the time goes in v1:
time: 143 us
  waiting for transfers between devices  67.7 us (47%)
  starting transfers between devices  42 us (29%)
  blocking collectives  12 us (8%)
  local copies, waits for them, and re-layouts  10.7 us (7%)
  matrix products  8.41 us (6%)
    all_to_all x1, waiting for transfers between devices, shards(): h = lax.all_to_all(spectrum, 'tm', 4, 1, tiled=True)  27.1 us
    all_to_all x1, starting transfers between devices, shards(): pair = lax.all_to_all(pair, 'tm', 3, 1, tiled=True)  17.7 us
    all_to_all x1, waiting for transfers between devices, shards(): pair = lax.all_to_all(pair, 'tm', 3, 1, tiled=True)  16.1 us
    all_to_all x1, waiting for transfers between devices, shards(): gated = lax.all_to_all(gated[:, :, None], 'tm', 0, 2, tiled=True)  14.3 us
    all_gather x1, blocking collectives, shards(): lax.all_gather(series, 'chan', axis=1, tiled=True)  12 us
    unnamed x43, local copies, waits for them, and re-layouts  8.48 us
    all_to_all x1, starting transfers between devices, shards(): gated = lax.all_to_all(gated[:, :, None], 'tm', 0, 2, tiled=True)  6.77 us
    all_to_all x1, starting transfers between devices, shards(): h = lax.all_to_all(spectrum, 'tm', 4, 1, tiled=True)  6.1 us
  transfers between devices with their start and end apart: 7, of which 7 were waited for; matrix products, arithmetic and copies ran while one was open for 3% of the time, Pallas kernels for 0%

profile of v1, /device:TPU:32, one launch (start us, length us, event | category | flops | bytes accessed | tf_op | source)
XLA Modules:
  0.0 142.6 jit_solution(12518707132341514371)
XLA Ops:
  0.0 1.2 copy.32
  1.3 12.0 %all_gather.3 = bf16[256,512]{1,0:T(8,128)(2,1)S(1)} all-gather(bf16[256,128]{1,0:T(8,128)(2,1)S(1)} %copy-done.13), channel_id=1, replica_groups=mesh['tm'=128,'chan'=4] {'chan'}, dimensions={1}, use_global_device_ids=true | all-gather | bytes 327680 | tf_op jit(solution)/shard_map/all_gather | solution.py:123
  13.3 0.3 fusion
  13.6 1.9 %collective-permute-start = (bf16[2,3,128]{2,0,1:T(2,128)(2,1)S(1)}, bf16[2,3,128]{2,0,1:T(2,128)(2,1)S(1)}, u32[]{:S(2)}, u32[]{:S(2)}) collective-permute-start(bf16[2,3,128]{2,0,1:T(2,128)(2,1)S(1)} %slice.63), channel_id=1, source_target_pairs={{0,4},{4,8},{8,12},{12,16},{16,20},{20,24},{24,28},{28,32},{32,36}... | collective-permute-start | bytes 4616 | tf_op jit(solution)/shard_map/ppermute | solution.py:44
  15.5 5.1 %collective-permute-done = bf16[2,3,128]{2,0,1:T(2,128)(2,1)S(1)} collective-permute-done((bf16[2,3,128]{2,0,1:T(2,128)(2,1)S(1)}, bf16[2,3,128]{2,0,1:T(2,128)(2,1)S(1)}, u32[]{:S(2)}, u32[]{:S(2)}) %collective-permute-start) | collective-permute-done | bytes 1568 | tf_op jit(solution)/shard_map/ppermute | solution.py:44
  20.7 0.7 copy-done.16
  21.3 0.1 fusion.9
  21.6 0.8 copy.33
  22.4 17.7 %all-to-all-start.1 = ((bf16[2,1,256,128]{2,0,1,3:T(2,128)(2,1)}), bf16[2,1,256,128]{2,0,1,3:T(2,128)(2,1)S(1)}, u32[]{:S(2)}, u32[]{:S(2)}) async-start(bf16[2,1,256,128]{2,0,1,3:T(2,128)(2,1)} %copy.33), calls=%async_computation.1 | async-start | bytes 262144 | tf_op jit(solution)/shard_map/all_to_all | solution.py:144
  40.1 1.0 copy.31
  41.1 16.1 %all-to-all-done.1 = bf16[2,1,256,128]{2,0,1,3:T(2,128)(2,1)S(1)} async-done(((bf16[2,1,256,128]{2,0,1,3:T(2,128)(2,1)}), bf16[2,1,256,128]{2,0,1,3:T(2,128)(2,1)S(1)}, u32[]{:S(2)}, u32[]{:S(2)}) %all-to-all-start.1) | async-done | bytes 131104 | tf_op jit(solution)/shard_map/all_to_all | solution.py:144
  57.2 6.1 %all-to-all-start = ((f32[2,1,2,256,128]{3,2,1,0,4:T(2,128)}), f32[2,1,2,256,128]{3,2,1,0,4:T(2,128)S(1)}, u32[]{:S(2)}, u32[]{:S(2)}) async-start(f32[2,1,2,256,128]{3,2,1,0,4:T(2,128)} %copy.31), calls=%async_computation | async-start | bytes 1048576 | tf_op jit(solution)/shard_map/all_to_all | solution.py:147
  63.3 0.6 copy-done.18
  64.0 0.6 dynamic_slice.7
  64.7 0.8 copy-done.11
  65.5 0.3 convolution_negate_fusion
  65.8 0.3 fusion.25
  66.1 0.4 copy-done.3
  66.5 0.2 copy-done.2
  66.8 0.4 fusion.22
  67.2 0.5 copy-done.1
  67.8 1.1 fusion.23
  68.9 0.4 convolution_add_fusion.2
  69.3 27.1 %all-to-all-done = f32[2,1,2,256,128]{3,2,1,0,4:T(2,128)S(1)} async-done(((f32[2,1,2,256,128]{3,2,1,0,4:T(2,128)}), f32[2,1,2,256,128]{3,2,1,0,4:T(2,128)S(1)}, u32[]{:S(2)}, u32[]{:S(2)}) %all-to-all-start) | async-done | bytes 524320 | tf_op jit(solution)/shard_map/all_to_all | solution.py:147
  96.5 0.2 fusion.27
  96.6 0.2 squeeze.23
  96.8 0.2 squeeze.21
  97.0 0.8 copy-done.7
  97.8 1.4 multiply_subtract_fusion
  99.2 0.4 fusion.29
  99.5 0.4 fusion.28
  99.9 0.4 convolution_add_fusion.1
  100.3 0.4 convolution_subtract_fusion
  100.7 0.5 copy-done.9
  101.2 0.6 fusion.17
  101.8 0.3 copy-done.12
  102.1 1.2 fusion.7
  103.5 0.5 broadcast.8
  104.0 1.0 reduce
  105.0 0.7 reshape.54
  105.7 6.8 %all-to-all-start.2 = ((bf16[128,2,128]{2,1,0:T(2,128)(2,1)}), bf16[128,2,128]{2,1,0:T(2,128)(2,1)S(1)}, u32[]{:S(2)}, u32[]{:S(2)}) async-start(bf16[128,2,128]{2,1,0:T(2,128)(2,1)} %reshape.54), calls=%async_computation.2 | async-start | bytes 131072 | tf_op jit(solution)/shard_map/all_to_all | solution.py:153
  112.5 14.3 %all-to-all-done.2 = bf16[128,2,128]{2,1,0:T(2,128)(2,1)S(1)} async-done(((bf16[128,2,128]{2,1,0:T(2,128)(2,1)}), bf16[128,2,128]{2,1,0:T(2,128)(2,1)S(1)}, u32[]{:S(2)}, u32[]{:S(2)}) %all-to-all-start.2) | async-done | bytes 65568 | tf_op jit(solution)/shard_map/all_to_all | solution.py:153
  126.9 3.6 %collective-permute-start.1 = (bf16[256,128]{0,1:T(8,128)(2,1)S(1)}, bf16[256,128]{0,1:T(8,128)(2,1)S(1)}, u32[]{:S(2)}, u32[]{:S(2)}) collective-permute-start(bf16[256,128]{0,1:T(8,128)(2,1)S(1)} %get-tuple-element.6), channel_id=1, source_target_pairs={{0,1},{1,2},{2,3},{3,0},{4,5},{5,6},{6,7},{7,4},{8,9},{9,10},{10,1... | collective-permute-start | bytes 196616 | tf_op jit(solution)/shard_map/ppermute | solution.py:26
  130.6 3.4 %collective-permute-start.2 = (bf16[256,128]{0,1:T(8,128)(2,1)S(1)}, bf16[256,128]{0,1:T(8,128)(2,1)S(1)}, u32[]{:S(2)}, u32[]{:S(2)}) collective-permute-start(bf16[256,128]{0,1:T(8,128)(2,1)S(1)} %get-tuple-element.6), channel_id=1, source_target_pairs={{0,3},{1,0},{2,1},{3,2},{4,7},{5,4},{6,5},{7,6},{8,11},{9,8},{10,9... | collective-permute-start | bytes 196616 | tf_op jit(solution)/shard_map/ppermute | solution.py:31
  134.0 0.2 collective-permute-done.1
  134.3 2.4 %collective-permute-start.3 = (bf16[256,128]{0,1:T(8,128)(2,1)S(1)}, bf16[256,128]{0,1:T(8,128)(2,1)S(1)}, u32[]{:S(2)}, u32[]{:S(2)}) collective-permute-start(bf16[256,128]{0,1:T(8,128)(2,1)S(1)} %collective-permute-done.1), channel_id=1, source_target_pairs={{0,1},{1,2},{2,3},{3,0},{4,5},{5,6},{6,7},{7,4},{8,9},{9,10},{10,1... | collective-permute-start | bytes 196616 | tf_op jit(solution)/shard_map/ppermute | solution.py:26
  136.8 4.9 %collective-permute-done.3 = bf16[256,128]{0,1:T(8,128)(2,1)S(1)} collective-permute-done((bf16[256,128]{0,1:T(8,128)(2,1)S(1)}, bf16[256,128]{0,1:T(8,128)(2,1)S(1)}, u32[]{:S(2)}, u32[]{:S(2)}) %collective-permute-start.3) | collective-permute-done | bytes 65568 | tf_op jit(solution)/shard_map/ppermute | solution.py:26
  141.7 0.9 fusion.6
  (44 shorter events, 0.7 us)
Async XLA Ops:
  0.0 141.6 %copy-start = (bf16[512,512]{1,0:T(8,128)(2,1)S(1)}, bf16[512,512]{1,0:T(8,128)(2,1)}, u32[]{:S(2)}) copy-start(bf16[512,512]{1,0:T(8,128)(2,1)} %param.22) | copy-start | bytes 1572868
  0.0 1.2 copy-start.13
  1.2 12.0 %copy-start.15 = (f32[3,128]{1,0:T(4,128)S(1)}, f32[3,128]{1,0:T(4,128)}, u32[]{:S(2)}) copy-start(f32[3,128]{1,0:T(4,128)} %param.17) | copy-start | bytes 4612
  13.3 2.3 %copy-start.14 = (f32[3,3,128]{2,1,0:T(4,128)S(1)}, f32[3,3,128]{2,1,0:T(4,128)}, u32[]{:S(2)}) copy-start(f32[3,3,128]{2,1,0:T(4,128)} %param.18) | copy-start | bytes 13828
  13.6 7.0 %collective-permute-start = (bf16[2,3,128]{2,0,1:T(2,128)(2,1)S(1)}, bf16[2,3,128]{2,0,1:T(2,128)(2,1)S(1)}, u32[]{:S(2)}, u32[]{:S(2)}) collective-permute-start(bf16[2,3,128]{2,0,1:T(2,128)(2,1)S(1)} %slice.63), channel_id=1, source_target_pairs={{0,4},{4,8},{8,12},{12,16},{16,20},{20,24},{24,28},{28,32},{32,36}... | collective-permute-start | bytes 4616 | tf_op jit(solution)/shard_map/ppermute | solution.py:44
  20.7 0.7 copy-start.16
  21.5 18.6 %copy-start.10 = (f32[2,1,2,256,128]{4,3,2,1,0:T(8,128)S(1)}, f32[2,1,2,256,128]{4,3,2,1,0:T(8,128)}, u32[]{:S(2)}) copy-start(f32[2,1,2,256,128]{4,3,2,1,0:T(8,128)} %param.20) | copy-start | bytes 1572868
  22.4 34.8 %all-to-all-start.1 = ((bf16[2,1,256,128]{2,0,1,3:T(2,128)(2,1)}), bf16[2,1,256,128]{2,0,1,3:T(2,128)(2,1)S(1)}, u32[]{:S(2)}, u32[]{:S(2)}) async-start(bf16[2,1,256,128]{2,0,1,3:T(2,128)(2,1)} %copy.33), calls=%async_computation.1 | async-start | bytes 262144 | tf_op jit(solution)/shard_map/all_to_all | solution.py:144
  57.2 39.3 %all-to-all-start = ((f32[2,1,2,256,128]{3,2,1,0,4:T(2,128)}), f32[2,1,2,256,128]{3,2,1,0,4:T(2,128)S(1)}, u32[]{:S(2)}, u32[]{:S(2)}) async-start(f32[2,1,2,256,128]{3,2,1,0,4:T(2,128)} %copy.31), calls=%async_computation | async-start | bytes 1048576 | tf_op jit(solution)/shard_map/all_to_all | solution.py:147
  63.3 0.7 copy-start.18
  64.6 0.9 copy-start.11
  64.6 1.2 copy-start.8
  65.5 1.0 copy-start.3
  65.5 1.0 copy-start.6
  65.8 1.0 copy-start.2
  66.8 0.9 copy-start.1
  66.8 1.0 copy-start.5
  67.8 1.1 copy-start.4
  96.8 1.0 copy-start.7
  100.3 0.9 copy-start.9
  101.2 0.9 copy-start.12
  105.7 21.1 %all-to-all-start.2 = ((bf16[128,2,128]{2,1,0:T(2,128)(2,1)}), bf16[128,2,128]{2,1,0:T(2,128)(2,1)S(1)}, u32[]{:S(2)}, u32[]{:S(2)}) async-start(bf16[128,2,128]{2,1,0:T(2,128)(2,1)} %reshape.54), calls=%async_computation.2 | async-start | bytes 131072 | tf_op jit(solution)/shard_map/all_to_all | solution.py:153
  126.9 7.4 %collective-permute-start.1 = (bf16[256,128]{0,1:T(8,128)(2,1)S(1)}, bf16[256,128]{0,1:T(8,128)(2,1)S(1)}, u32[]{:S(2)}, u32[]{:S(2)}) collective-permute-start(bf16[256,128]{0,1:T(8,128)(2,1)S(1)} %get-tuple-element.6), channel_id=1, source_target_pairs={{0,1},{1,2},{2,3},{3,0},{4,5},{5,6},{6,7},{7,4},{8,9},{9,10},{10,1... | collective-permute-start | bytes 196616 | tf_op jit(solution)/shard_map/ppermute | solution.py:26
  130.6 6.2 %collective-permute-start.2 = (bf16[256,128]{0,1:T(8,128)(2,1)S(1)}, bf16[256,128]{0,1:T(8,128)(2,1)S(1)}, u32[]{:S(2)}, u32[]{:S(2)}) collective-permute-start(bf16[256,128]{0,1:T(8,128)(2,1)S(1)} %get-tuple-element.6), channel_id=1, source_target_pairs={{0,3},{1,0},{2,1},{3,2},{4,7},{5,4},{6,5},{7,6},{8,11},{9,8},{10,9... | collective-permute-start | bytes 196616 | tf_op jit(solution)/shard_map/ppermute | solution.py:31
  134.3 7.4 %collective-permute-start.3 = (bf16[256,128]{0,1:T(8,128)(2,1)S(1)}, bf16[256,128]{0,1:T(8,128)(2,1)S(1)}, u32[]{:S(2)}, u32[]{:S(2)}) collective-permute-start(bf16[256,128]{0,1:T(8,128)(2,1)S(1)} %collective-permute-done.1), channel_id=1, source_target_pairs={{0,1},{1,2},{2,3},{3,0},{4,5},{5,6},{6,7},{7,4},{8,9},{9,10},{10,1... | collective-permute-start | bytes 196616 | tf_op jit(solution)/shard_map/ppermute | solution.py:26
  136.8 4.9 %copy-start.17 = (f32[128]{0:T(128)S(1)}, f32[128]{0:T(128)}, u32[]{:S(2)}) copy-start(f32[128]{0:T(128)} %param.23) | copy-start | bytes 1540
